TPU v7x, 512 devices: a whole 4x8x8 slice. The times are simulated.
512 devices in a mesh: dp: 8 (over z), expert: 64 (over y, x, core).
Axes of the slice: x: 4, y: 8, z: 8, core: 2. Of those that a mesh axis runs over, the one named last changes fastest.
Arguments:
- tokens: bfloat16 [65536, 1024], P(('dp', 'expert')), may hold values from -6 to 6
- expert_ids: int32 [65536, 4], P(('dp', 'expert')), may hold values from 0 to 63, all different within a row; in each aligned block of 128 rows (0 to 127, 128 to 255, ...) at most 16 rows name the same one
- gate_probs: float32 [65536, 4], P(('dp', 'expert')), may hold values from 0.05 to 1
- gate_up: bfloat16 [64, 1024, 768], P('expert', 'dp'), may hold values from -0.1875 to 0.1875
- down_proj: bfloat16 [64, 384, 1024], P('expert', None, 'dp'), may hold values from -0.3125 to 0.3125
- cotangent: bfloat16 [65536, 1024], P(('dp', 'expert')), may hold values from -0.75 to 0.75
Outputs:
- moe_out: bfloat16 [65536, 1024], P(('dp', 'expert'))
- token_grads: bfloat16 [65536, 1024], P(('dp', 'expert'))
- gate_grads: float32 [65536, 4], P(('dp', 'expert'))
- gate_up_grads: float32 [64, 1024, 768], P('expert', 'dp')
- down_grads: float32 [64, 384, 1024], P('expert', None, 'dp')
Inputs may be any that keep to these rules, and one draw needn't show every extreme that they name: `expert_ids`: each row names 4 different experts. Among the rows of one device no expert is named more than 16 times, and in every draw some device names some expert exactly 16 times.
All inputs are finite; a program needn't handle non-finite values.
Results may differ from a plain program's by a relative error of at most 0.012.
Values may be sent and summed in bfloat16 or wider, within the bound.
No kernel may reach another device: no remote copies, remote signals or barrier semaphores. Data moves between devices by JAX's collectives and lax.ppermute only.
A program may use at most 64 MiB of HBM per device.

v0:
```python
import jax
import jax.numpy as jnp
from jax import lax
from jax.sharding import PartitionSpec as P


def forward_rows(rows_in, weight_in, weight_out):
    hidden_width = weight_out.shape[0]
    pre_act = jnp.dot(rows_in, weight_in, preferred_element_type=jnp.float32)
    hidden = (jax.nn.silu(pre_act[:, :hidden_width]) * pre_act[:, hidden_width:]).astype(
        jnp.bfloat16
    )
    expert_out = jnp.dot(hidden, weight_out, preferred_element_type=jnp.float32).astype(
        jnp.bfloat16
    )
    return (expert_out, pre_act, hidden)


def backward_rows(rows_in, grad_rows, pre_act, hidden, weight_in, weight_out):
    hidden_width = weight_out.shape[0]
    contract_last = (((1,), (1,)), ((), ()))
    contract_first = (((0,), (0,)), ((), ()))
    grad_hidden = lax.dot_general(
        grad_rows, weight_out, contract_last, preferred_element_type=jnp.float32
    )
    pre_gate = pre_act[:, :hidden_width]
    sigmoid_value = jax.nn.sigmoid(pre_gate)
    grad_gate = (
        grad_hidden
        * pre_act[:, hidden_width:]
        * sigmoid_value
        * (1.0 + pre_gate * (1.0 - sigmoid_value))
    )
    grad_up = grad_hidden * jax.nn.silu(pre_gate)
    grad_pre = jnp.concatenate([grad_gate, grad_up], axis=1).astype(jnp.bfloat16)
    grad_in = lax.dot_general(
        grad_pre, weight_in, contract_last, preferred_element_type=jnp.float32
    ).astype(jnp.bfloat16)
    weight_in_grad = lax.dot_general(
        rows_in, grad_pre, contract_first, preferred_element_type=jnp.float32
    )
    weight_out_grad = lax.dot_general(
        hidden, grad_rows, contract_first, preferred_element_type=jnp.float32
    )
    return (grad_in, weight_in_grad, weight_out_grad)


def live_slots(recv_counts, capacity):
    within = jnp.arange(capacity, dtype=jnp.int32)[None, :] < recv_counts[:, None]
    return within.reshape(-1)


def expert_forward(rows_in, filled, weight_in, weight_out):
    zero_row = jnp.zeros((), jnp.bfloat16)
    expert_out, pre_act, hidden = forward_rows(rows_in, weight_in, weight_out)
    expert_out = jnp.where(filled[:, None], expert_out, zero_row)
    stored = (rows_in, pre_act, hidden, None)
    return (expert_out, stored)


def expert_backward(grads_in, filled, stored, weight_in, weight_out):
    zero_row = jnp.zeros((), jnp.bfloat16)
    rows_in, pre_act, hidden, unused_plan = stored
    grad_back, in_grad, out_grad = backward_rows(
        rows_in, grads_in, pre_act, hidden, weight_in, weight_out
    )
    grad_back = jnp.where(filled[:, None], grad_back, zero_row)
    return (grad_back, in_grad, out_grad)


def local(tokens, expert_ids, gate_probs, gate_up, down_proj, cotangent):
    token_count, top_count = expert_ids.shape
    expert_count = lax.axis_size("expert")
    capacity = 2 * token_count * top_count // expert_count
    route_count = token_count * top_count
    slot_count = expert_count * capacity
    flat_ids = expert_ids.reshape(route_count)
    onehot = (flat_ids[:, None] == jnp.arange(expert_count, dtype=jnp.int32)[None, :]).astype(
        jnp.int32
    )
    slot_index = jnp.sum((jnp.cumsum(onehot, axis=0) - onehot) * onehot, axis=1)
    position = flat_ids * capacity + slot_index
    counts = jnp.sum(onehot, axis=0)
    slot_range = jnp.arange(slot_count, dtype=jnp.int32)
    matches = position[None, :] == slot_range[:, None]
    route_of_slot = jnp.sum(
        jnp.where(matches, jnp.arange(route_count, dtype=jnp.int32)[None, :], 0), axis=1
    )
    slot_filled = jnp.any(matches, axis=1)
    token_of_slot = route_of_slot // top_count
    zero_row = jnp.zeros((), jnp.bfloat16)
    send_tokens = jnp.where(slot_filled[:, None], tokens[token_of_slot], zero_row)
    slot_probs = jnp.where(slot_filled, gate_probs.reshape(route_count)[route_of_slot], 0.0)
    send_grads = (slot_probs[:, None] * cotangent[token_of_slot].astype(jnp.float32)).astype(
        jnp.bfloat16
    )
    weight_in, weight_out = (
        lax.all_gather(gate_up, "dp", axis=1, tiled=True),
        lax.all_gather(down_proj, "dp", axis=2, tiled=True),
    )
    weight_in = weight_in[0]
    weight_out = weight_out[0]
    rows_in, recv_counts = (
        lax.all_to_all(send_tokens, "expert", split_axis=0, concat_axis=0, tiled=True),
        lax.all_to_all(counts, "expert", split_axis=0, concat_axis=0, tiled=True),
    )
    filled = live_slots(recv_counts, capacity)
    expert_out, stored = expert_forward(rows_in, filled, weight_in, weight_out)
    back_out = lax.all_to_all(expert_out, "expert", split_axis=0, concat_axis=0, tiled=True)
    grads_in = lax.all_to_all(send_grads, "expert", split_axis=0, concat_axis=0, tiled=True)
    grad_back, in_grad, out_grad = expert_backward(grads_in, filled, stored, weight_in, weight_out)
    back_grad = lax.all_to_all(grad_back, "expert", split_axis=0, concat_axis=0, tiled=True)
    sum_in, sum_out = (
        lax.psum_scatter(
            in_grad[None].astype(jnp.bfloat16), "dp", scatter_dimension=1, tiled=True
        ).astype(jnp.float32),
        lax.psum_scatter(
            out_grad[None].astype(jnp.bfloat16), "dp", scatter_dimension=2, tiled=True
        ).astype(jnp.float32),
    )
    out_routes = back_out[position].reshape(token_count, top_count, -1).astype(jnp.float32)
    moe_out = jnp.sum(gate_probs[:, :, None] * out_routes, axis=1).astype(jnp.bfloat16)
    gate_grads = jnp.sum(cotangent.astype(jnp.float32)[:, None, :] * out_routes, axis=2)
    grad_routes = back_grad[position].reshape(token_count, top_count, -1).astype(jnp.float32)
    token_grads = jnp.sum(grad_routes, axis=1).astype(jnp.bfloat16)
    return (moe_out, token_grads, gate_grads, sum_in, sum_out)


def solution(mesh):
    return jax.shard_map(
        local,
        mesh=mesh,
        in_specs=(
            P(("dp", "expert"), None),
            P(("dp", "expert"), None),
            P(("dp", "expert"), None),
            P("expert", "dp", None),
            P("expert", None, "dp"),
            P(("dp", "expert"), None),
        ),
        out_specs=(
            P(("dp", "expert"), None),
            P(("dp", "expert"), None),
            P(("dp", "expert"), None),
            P("expert", "dp", None),
            P("expert", None, "dp"),
        ),
        check_vma=False,
    )
```

profile of v0, /device:TPU:2, one launch (start us, length us, event | category | flops | bytes accessed | tf_op | source)
XLA Modules:
  0.0 300.2 jit_solution(8653985739572995588)
XLA Ops:
  8.2 1.2 reduce-window.6
  10.6 10.7 %all-to-all-start = ((s32[64,1,1]{2,1,0:T(1,128)}), s32[64,1,1]{2,1,0:T(1,128)S(1)}, u32[]{:S(2)}, u32[]{:S(2)}) async-start(s32[64,1,1]{2,1,0:T(1,128)} %copy.36), calls=%async_computation | async-start | bytes 65536 | tf_op jit(solution)/shard_map/all_to_all | solution.py:105
  22.0 4.1 %gather_fusion = bf16[1024,1024]{1,0:T(8,128)(2,1)S(1)} fusion(bf16[128,1024]{1,0:T(8,128)(2,1)S(1)} %copy-done, s32[1024]{0:T(1024)S(1)} %broadcast_clamp_fusion.1), kind=kCustom, calls=%fused_computation | custom fusion | bytes 4198400 | tf_op jit(solution)/shard_map/gather | solution.py:92
  26.1 1.6 broadcast_select_fusion
  27.7 2.2 all-to-all-done
  29.8 8.5 %all-to-all-start.1 = ((bf16[64,16,1024]{2,1,0:T(8,128)(2,1)}), bf16[64,16,1024]{2,1,0:T(8,128)(2,1)}, u32[]{:S(2)}, u32[]{:S(2)}) async-start(bf16[64,16,1024]{2,1,0:T(8,128)(2,1)} %broadcast_select_fusion), calls=%async_computation.1 | async-start | bytes 4194304 | tf_op jit(solution)/shard_map/all_to_all | solution.py:104
  38.5 6.9 %gather_fusion.2 = f32[1024]{0:T(1024)S(1)} fusion(f32[512]{0:T(512)S(1)} %reshape.204, s32[1024]{0:T(1024)S(1)} %broadcast_clamp_fusion), kind=kCustom, calls=%fused_computation.2 | custom fusion | bytes 12288 | tf_op jit(solution)/shard_map/gather | solution.py:93
  45.5 4.1 %gather_fusion.3 = bf16[1024,1024]{1,0:T(8,128)(2,1)S(1)} fusion(bf16[128,1024]{1,0:T(8,128)(2,1)S(1)} %copy-done.1, s32[1024]{0:T(1024)S(1)} %broadcast_clamp_fusion.1), kind=kCustom, calls=%fused_computation.3 | custom fusion | bytes 4198400 | tf_op jit(solution)/shard_map/gather | solution.py:94
  49.6 1.8 fusion
  51.4 38.1 %all-to-all-done.1 = bf16[64,16,1024]{2,1,0:T(8,128)(2,1)} async-done(((bf16[64,16,1024]{2,1,0:T(8,128)(2,1)}), bf16[64,16,1024]{2,1,0:T(8,128)(2,1)}, u32[]{:S(2)}, u32[]{:S(2)}) %all-to-all-start.1) | async-done | bytes 2097184 | tf_op jit(solution)/shard_map/all_to_all | solution.py:104
  89.4 5.4 %all-to-all-start.3 = ((bf16[64,16,1024]{2,1,0:T(8,128)(2,1)}), bf16[64,16,1024]{2,1,0:T(8,128)(2,1)S(1)}, u32[]{:S(2)}, u32[]{:S(2)}) async-start(bf16[64,16,1024]{2,1,0:T(8,128)(2,1)} %fusion), calls=%async_computation.3 | async-start | bytes 4194304 | tf_op jit(solution)/shard_map/all_to_all | solution.py:110
  95.6 34.6 %all_gather.7 = bf16[1,384,1024]{2,1,0:T(8,128)(2,1)S(1)} all-gather(bf16[1,384,128]{2,1,0:T(8,128)(2,1)} %param.10), channel_id=1, replica_groups=mesh['dp'=8,'expert'=64] {'dp'}, dimensions={2}, use_global_device_ids=true | all-gather | bytes 884736 | tf_op jit(solution)/shard_map/all_gather | solution.py:99
  130.2 1.2 reduce.5
  131.6 15.3 %all-gather.2.cloned.1.call-done = bf16[1,1024,768]{2,1,0:T(8,128)(2,1)} async-done(((bf16[1,128,768]{2,1,0:T(8,128)(2,1)}), bf16[1,1024,768]{2,1,0:T(8,128)(2,1)}) %all-gather.2.cloned.1.call-update) | async-done | bytes 1572880 | tf_op jit(solution)/shard_map/all_gather | solution.py:98
  146.9 5.5 %fusion.3 = f32[1024,768]{0,1:T(8,128)} fusion(bf16[1024,1024]{1,0:T(8,128)(2,1)} %bitcast.5, bf16[1,1024,768]{2,1,0:T(8,128)(2,1)} %all-gather.2.cloned.1.call-done), kind=kOutput, calls=%fused_computation.18 | convolution fusion | flops 1610612736 | bytes 6815744 | tf_op jit(solution)/shard_map/dot_general | solution.py:9
  152.5 5.1 %multiply_convert_fusion.1 = (bf16[1024,384]{0,1:T(8,128)(2,1)S(1)}, bf16[1024,384]{0,1:T(8,128)(2,1)S(1)}, bf16[1024,384]{0,1:T(8,128)(2,1)}) fusion(f32[1024,768]{0,1:T(8,128)} %fusion.3, bf16[1024,1024]{1,0:T(8,128)(2,1)S(1)} %bitcast.60, bf16[1,384,1024]{2,1,0:T(8,128)(2,1)S(1)} %all_gather.7), kind=kOutput, calls=%fused_computation.21 | convolution fusion | flops 811204608 | bytes 8388608 | tf_op jit(solution)/shard_map/dot_general | solution.py:23
  157.6 3.3 %convert_select_fusion = bf16[1024,1024]{1,0:T(8,128)(2,1)} fusion(pred[1024]{0:T(1024)(128)(4,1)S(1)} %lt.50, bf16[1,1024,768]{2,1,0:T(8,128)(2,1)S(1)} %copy-done.6, bf16[1024,384]{0,1:T(8,128)(2,1)S(1)} %get-tuple-element.25, bf16[1024,384]{0,1:T(8,128)(2,1)S(1)} %get-tuple-element.24), kind=kOutput, calls=%fused_computation.8 | convolution fusion | flops 1615855616 | bytes 5243904 | tf_op jit(solution)/shard_map/dot_general | solution.py:36
  160.9 10.3 %all-to-all-start.4 = ((bf16[64,16,1024]{2,1,0:T(8,128)(2,1)}), bf16[64,16,1024]{2,1,0:T(8,128)(2,1)S(1)}, u32[]{:S(2)}, u32[]{:S(2)}) async-start(bf16[64,16,1024]{2,1,0:T(8,128)(2,1)} %bitcast.62), calls=%async_computation.4 | async-start | bytes 4194304 | tf_op jit(solution)/shard_map/all_to_all | solution.py:112
  171.2 3.7 %fusion.7 = bf16[1,384,1024]{2,1,0:T(8,128)(2,1)} fusion(bf16[1024,384]{0,1:T(8,128)(2,1)} %get-tuple-element.26, bf16[1024,1024]{1,0:T(8,128)(2,1)} %bitcast.61), kind=kOutput, calls=%fused_computation.27 | convolution fusion | flops 805699584 | bytes 3670016 | tf_op jit(solution)/shard_map/dot_general | solution.py:42
  174.9 4.8 %copy.42 = bf16[1,384,1024]{1,0,2:T(2,128)(2,1)} copy(bf16[1,384,1024]{2,1,0:T(8,128)(2,1)} %fusion.7) | data formatting | bytes 1572864
  179.7 2.5 copy.48
  182.3 3.8 %convert_select_fusion.1 = bf16[1024,1024]{1,0:T(8,128)(2,1)} fusion(pred[1024]{0:T(1024)(128)(4,1)S(1)} %lt.50, bf16[1024,384]{0,1:T(8,128)(2,1)} %get-tuple-element.26, bf16[1,384,1024]{2,1,0:T(8,128)(2,1)S(1)} %all_gather.7), kind=kOutput, calls=%fused_computation.10 | convolution fusion | flops 807403520 | bytes 3671040 | tf_op jit(solution)/shard_map/dot_general | solution.py:13
  186.0 36.4 %all-to-all-done.4 = bf16[64,16,1024]{2,1,0:T(8,128)(2,1)S(1)} async-done(((bf16[64,16,1024]{2,1,0:T(8,128)(2,1)}), bf16[64,16,1024]{2,1,0:T(8,128)(2,1)S(1)}, u32[]{:S(2)}, u32[]{:S(2)}) %all-to-all-start.4) | async-done | bytes 2097184 | tf_op jit(solution)/shard_map/all_to_all | solution.py:112
  222.4 5.8 %all-to-all-start.2 = ((bf16[64,16,1024]{2,1,0:T(8,128)(2,1)}), bf16[64,16,1024]{2,1,0:T(8,128)(2,1)}, u32[]{:S(2)}, u32[]{:S(2)}) async-start(bf16[64,16,1024]{2,1,0:T(8,128)(2,1)} %bitcast.59), calls=%async_computation.2 | async-start | bytes 4194304 | tf_op jit(solution)/shard_map/all_to_all | solution.py:109
  228.5 4.8 %fusion.6 = bf16[1,1024,768]{2,1,0:T(8,128)(2,1)} fusion(bf16[1024,1024]{1,0:T(8,128)(2,1)} %bitcast.5, bf16[1024,384]{0,1:T(8,128)(2,1)} %copy-done.9, bf16[1024,384]{0,1:T(8,128)(2,1)S(1)} %copy-done.8), kind=kOutput, calls=%fused_computation.25 | convolution fusion | flops 1614544896 | bytes 5242880 | tf_op jit(solution)/shard_map/dot_general | solution.py:39
  236.3 38.8 %reduce-scatter.5.cloned.1.call-done = bf16[1,128,768]{2,1,0:T(8,128)(2,1)} async-done(((bf16[1,1024,768]{2,1,0:T(8,128)(2,1)}), bf16[1,128,768]{2,1,0:T(8,128)(2,1)}) %reduce-scatter.5.cloned.1.call-update) | async-done | bytes 196624 | tf_op jit(solution)/shard_map/reduce_scatter | solution.py:114
  275.1 1.7 convert_element_type.78
  276.8 2.8 gather_fusion.4
  279.6 2.3 reshape.205
  281.9 4.6 %gather_fusion.1 = bf16[512,1024]{1,0:T(8,128)(2,1)S(1)} fusion(bf16[1024,1024]{1,0:T(8,128)(2,1)} %bitcast.9, s32[1024]{0:T(1024)S(1)} %pad_clamp_fusion), kind=kCustom, calls=%fused_computation.1 | custom fusion | bytes 2099200 | tf_op jit(solution)/shard_map/gather | solution.py:121
  287.2 3.7 %multiply_reduce_fusion = (f32[128,4]{1,0:T(8,128)S(1)}, bf16[128,1024]{1,0:T(8,128)(2,1)}) fusion(f32[128,4,1024]{2,1,0:T(4,128)S(1)} %reshape.206, f32[128,1024]{1,0:T(8,128)} %convert_element_type.75, f32[128,4]{1,0:T(8,128)S(1)} %copy.34), kind=kLoop, calls=%fused_computation.7 | loop fusion | flops 1965568 | bytes 2887680 | tf_op jit(solution)/shard_map/reduce_sum | solution.py:123
  291.5 2.1 reduce_sum.67
  (62 shorter events, 8.8 us)
Async XLA Ops:
  7.2 14.8 %copy-start = (bf16[128,1024]{1,0:T(8,128)(2,1)S(1)}, bf16[128,1024]{1,0:T(8,128)(2,1)}, u32[]{:S(2)}) copy-start(bf16[128,1024]{1,0:T(8,128)(2,1)} %param.6) | copy-start | bytes 786436
  10.6 19.2 %all-to-all-start = ((s32[64,1,1]{2,1,0:T(1,128)}), s32[64,1,1]{2,1,0:T(1,128)S(1)}, u32[]{:S(2)}, u32[]{:S(2)}) async-start(s32[64,1,1]{2,1,0:T(1,128)} %copy.36), calls=%async_computation | async-start | bytes 65536 | tf_op jit(solution)/shard_map/all_to_all | solution.py:105
  27.7 10.6 %copy-start.5 = (f32[128,4]{0,1:T(4,128)S(1)}, f32[128,4]{0,1:T(4,128)}, u32[]{:S(2)}) copy-start(f32[128,4]{0,1:T(4,128)} %param.8) | copy-start | bytes 6148
  29.8 59.6 %all-to-all-start.1 = ((bf16[64,16,1024]{2,1,0:T(8,128)(2,1)}), bf16[64,16,1024]{2,1,0:T(8,128)(2,1)}, u32[]{:S(2)}, u32[]{:S(2)}) async-start(bf16[64,16,1024]{2,1,0:T(8,128)(2,1)} %broadcast_select_fusion), calls=%async_computation.1 | async-start | bytes 4194304 | tf_op jit(solution)/shard_map/all_to_all | solution.py:104
  38.5 7.0 %copy-start.1 = (bf16[128,1024]{1,0:T(8,128)(2,1)S(1)}, bf16[128,1024]{1,0:T(8,128)(2,1)}, u32[]{:S(2)}) copy-start(bf16[128,1024]{1,0:T(8,128)(2,1)} %param.11) | copy-start | bytes 786436
  89.4 63.0 %all-to-all-start.3 = ((bf16[64,16,1024]{2,1,0:T(8,128)(2,1)}), bf16[64,16,1024]{2,1,0:T(8,128)(2,1)S(1)}, u32[]{:S(2)}, u32[]{:S(2)}) async-start(bf16[64,16,1024]{2,1,0:T(8,128)(2,1)} %fusion), calls=%async_computation.3 | async-start | bytes 4194304 | tf_op jit(solution)/shard_map/all_to_all | solution.py:110
  94.9 52.0 %all-gather.2.cloned.1.call-start = ((), (), s32[]{:S(2)}) async-start(), calls=%async_computation.7 | async-start | bytes 1769472 | tf_op jit(solution)/shard_map/all_gather | solution.py:98
  152.5 5.1 %copy-start.3 = (bf16[64,16,1024]{2,1,0:T(8,128)(2,1)}, bf16[64,16,1024]{2,1,0:T(8,128)(2,1)S(1)}, u32[]{:S(2)}) copy-start(bf16[64,16,1024]{2,1,0:T(8,128)(2,1)S(1)} %all-to-all-done.3) | copy-start | bytes 6291460
  152.5 5.1 %copy-start.6 = (bf16[1,1024,768]{2,1,0:T(8,128)(2,1)S(1)}, bf16[1,1024,768]{2,1,0:T(8,128)(2,1)}, u32[]{:S(2)}) copy-start(bf16[1,1024,768]{2,1,0:T(8,128)(2,1)} %all-gather.2.cloned.1.call-done) | copy-start | bytes 4718596
  157.6 3.3 %copy-start.7 = (bf16[1024,384]{0,1:T(8,128)(2,1)}, bf16[1024,384]{0,1:T(8,128)(2,1)S(1)}, u32[]{:S(2)}) copy-start(bf16[1024,384]{0,1:T(8,128)(2,1)S(1)} %get-tuple-element.24) | copy-start | bytes 2359300
  157.6 3.3 %copy-start.9 = (bf16[1024,384]{0,1:T(8,128)(2,1)}, bf16[1024,384]{0,1:T(8,128)(2,1)S(1)}, u32[]{:S(2)}) copy-start(bf16[1024,384]{0,1:T(8,128)(2,1)S(1)} %get-tuple-element.25) | copy-start | bytes 2359300
  160.9 61.5 %all-to-all-start.4 = ((bf16[64,16,1024]{2,1,0:T(8,128)(2,1)}), bf16[64,16,1024]{2,1,0:T(8,128)(2,1)S(1)}, u32[]{:S(2)}, u32[]{:S(2)}) async-start(bf16[64,16,1024]{2,1,0:T(8,128)(2,1)} %bitcast.62), calls=%async_computation.4 | async-start | bytes 4194304 | tf_op jit(solution)/shard_map/all_to_all | solution.py:112
  171.2 63.3 %reduce-scatter.7.cloned.1.call-start = ((), (), s32[]{:S(2)}) async-start(), calls=%async_computation.9 | async-start | bytes 884736
  222.4 6.0 %copy-start.8 = (bf16[1024,384]{0,1:T(8,128)(2,1)S(1)}, bf16[1024,384]{0,1:T(8,128)(2,1)}, u32[]{:S(2)}) copy-start(bf16[1024,384]{0,1:T(8,128)(2,1)} %copy-done.7) | copy-start | bytes 2359300
  222.4 59.4 %all-to-all-start.2 = ((bf16[64,16,1024]{2,1,0:T(8,128)(2,1)}), bf16[64,16,1024]{2,1,0:T(8,128)(2,1)}, u32[]{:S(2)}, u32[]{:S(2)}) async-start(bf16[64,16,1024]{2,1,0:T(8,128)(2,1)} %bitcast.59), calls=%async_computation.2 | async-start | bytes 4194304 | tf_op jit(solution)/shard_map/all_to_all | solution.py:109
  228.2 46.9 %reduce-scatter.5.cloned.1.call-start = ((), (), s32[]{:S(2)}) async-start(), calls=%async_computation.8 | async-start | bytes 1769472 | tf_op jit(solution)/shard_map/reduce_scatter | solution.py:114
  233.3 0.9 copy-start.4
  287.2 4.4 %copy-start.2 = (bf16[128,4,1024]{2,1,0:T(4,128)(2,1)S(1)}, bf16[128,4,1024]{2,1,0:T(4,128)(2,1)}, u32[]{:S(2)}) copy-start(bf16[128,4,1024]{2,1,0:T(4,128)(2,1)} %reshape.205) | copy-start | bytes 3145732
Sparse Core Ops, SparseCore 0:
  97.8 49.0 all-gather.1
  182.4 39.1 reduce-scatter.6
  233.4 41.6 reduce-scatter.4
where the time goes:
time: 301 us; the launch traced here: 300 us
  waiting for transfers between devices  131 us (44%)
  starting transfers between devices  40.9 us (14%)
  local copies, waits for them, and re-layouts  37.2 us (12%)
  blocking collectives  34.6 us (11%)
  matrix products  26.3 us (9%)
  other arithmetic  15.8 us (5%)
  between operations  14 us (5%)
    reduce_scatter x1, waiting for transfers between devices, local(): lax.psum_scatter(in_grad[None].astype(jnp.bfloat16), 'dp', scatter_dimens...  38.8 us
    all_to_all x1, waiting for transfers between devices, local(): lax.all_to_all(send_tokens, 'expert', split_axis=0, concat_axis=0, tiled=...  38.1 us
    all_to_all x1, waiting for transfers between devices, local(): lax.all_to_all(grad_back, 'expert', split_axis=0, concat_axis=0, tiled=True)  36.4 us
    all_gather x1, blocking collectives, local(): lax.all_gather(down_proj, 'dp', axis=2, tiled=True)  34.6 us
    all_gather x1, waiting for transfers between devices, local(): lax.all_gather(gate_up, 'dp', axis=1, tiled=True)  15.3 us
    all_to_all x1, starting transfers between devices, local(): lax.all_to_all(counts, 'expert', split_axis=0, concat_axis=0, tiled=True)  10.7 us
    all_to_all x1, starting transfers between devices, local(): lax.all_to_all(grad_back, 'expert', split_axis=0, concat_axis=0, tiled=True)  10.3 us
    unnamed x27, local copies, waits for them, and re-layouts  10.1 us
  transfers between devices with their start and end apart: 8, of which 5 were waited for; matrix products, arithmetic and copies ran while one was open for 19% of the time, Pallas kernels for 0%

commit v1 on v0

--- a/solution.py
+++ b/solution.py
@@ -95,7 +95,9 @@
         jnp.bfloat16
     )
     weight_in, weight_out = (
-        lax.all_gather(gate_up, "dp", axis=1, tiled=True),
+        jnp.concatenate(
+            lax.all_to_all(jnp.stack([gate_up] * lax.axis_size("dp")), "dp", 0, 0), axis=1
+        ),
         lax.all_gather(down_proj, "dp", axis=2, tiled=True),
     )
     weight_in = weight_in[0]

time: 301 us -> 340 us (1.13)
  the two profiles are of different devices: /device:TPU:2 before, /device:TPU:4 now
where the time goes in v1:
time: 340 us; the launch traced here: 339 us
  waiting for transfers between devices  165 us (49%)
  blocking collectives  43.1 us (13%)
  local copies, waits for them, and re-layouts  38.7 us (11%)
  starting transfers between devices  34.4 us (10%)
  matrix products  28.2 us (8%)
  other arithmetic  15.8 us (5%)
  between operations  14.3 us (4%)
    all_to_all x1, waiting for transfers between devices, local(): lax.all_to_all(send_tokens, 'expert', split_axis=0, concat_axis=0, tiled=...  38.2 us
    reduce_scatter x1, waiting for transfers between devices, local(): lax.psum_scatter(in_grad[None].astype(jnp.bfloat16), 'dp', scatter_dimens...  37.1 us
    all_to_all x1, waiting for transfers between devices, local(): lax.all_to_all(grad_back, 'expert', split_axis=0, concat_axis=0, tiled=True)  36.4 us
    all_to_all x1, waiting for transfers between devices, local(): lax.all_to_all(jnp.stack([gate_up] * lax.axis_size('dp')), 'dp', 0, 0)  33.7 us
    all_gather x1, blocking collectives, local(): lax.all_gather(down_proj, 'dp', axis=2, tiled=True)  24.9 us
    all_to_all x1, waiting for transfers between devices, local(): lax.all_to_all(send_grads, 'expert', split_axis=0, concat_axis=0, tiled=T...  19.4 us
    all_to_all x1, blocking collectives, local(): lax.all_to_all(counts, 'expert', split_axis=0, concat_axis=0, tiled=True)  18.2 us
    all_to_all x1, starting transfers between devices, local(): lax.all_to_all(jnp.stack([gate_up] * lax.axis_size('dp')), 'dp', 0, 0)  10.3 us
  transfers between devices with their start and end apart: 7, of which 5 were waited for; matrix products, arithmetic and copies ran while one was open for 16% of the time, Pallas kernels for 0%

profile of v1, /device:TPU:4, one launch (start us, length us, event | category | flops | bytes accessed | tf_op | source)
XLA Modules:
  0.0 339.4 jit_solution(7914620953448433860)
XLA Ops:
  10.0 18.2 %all_to_all.56 = s32[64,1,1]{2,1,0:T(1,128)S(1)} all-to-all(s32[64,1,1]{2,1,0:T(1,128)S(1)} %copy.36), channel_id=1, replica_groups=mesh['dp'=8,'expert'=64] {'expert'}, dimensions={0} | all-to-all | bytes 512 | tf_op jit(solution)/shard_map/all_to_all | solution.py:107
  28.2 2.2 stack.2
  30.4 10.3 %all-to-all-start.2 = ((bf16[8,1,128,768]{3,2,1,0:T(8,128)(2,1)}), bf16[8,1,128,768]{3,2,1,0:T(8,128)(2,1)}, u32[]{:S(2)}, u32[]{:S(2)}) async-start(bf16[8,1,128,768]{3,2,1,0:T(8,128)(2,1)} %stack.2), calls=%async_computation.2 | async-start | bytes 3145728 | tf_op jit(solution)/shard_map/all_to_all | solution.py:99
  41.4 4.1 %gather_fusion = bf16[1024,1024]{1,0:T(8,128)(2,1)S(1)} fusion(bf16[128,1024]{1,0:T(8,128)(2,1)S(1)} %copy-done, s32[1024]{0:T(1024)S(1)} %broadcast_clamp_fusion.1), kind=kCustom, calls=%fused_computation | custom fusion | bytes 4198400 | tf_op jit(solution)/shard_map/gather | solution.py:92
  45.5 1.6 broadcast_select_fusion
  47.1 33.7 %all-to-all-done.2 = bf16[8,1,128,768]{3,2,1,0:T(8,128)(2,1)} async-done(((bf16[8,1,128,768]{3,2,1,0:T(8,128)(2,1)}), bf16[8,1,128,768]{3,2,1,0:T(8,128)(2,1)}, u32[]{:S(2)}, u32[]{:S(2)}) %all-to-all-start.2) | async-done | bytes 1572896 | tf_op jit(solution)/shard_map/all_to_all | solution.py:99
  80.8 7.2 %all-to-all-start.1 = ((bf16[64,16,1024]{2,1,0:T(8,128)(2,1)}), bf16[64,16,1024]{2,1,0:T(8,128)(2,1)}, u32[]{:S(2)}, u32[]{:S(2)}) async-start(bf16[64,16,1024]{2,1,0:T(8,128)(2,1)} %broadcast_select_fusion), calls=%async_computation.1 | async-start | bytes 4194304 | tf_op jit(solution)/shard_map/all_to_all | solution.py:106
  88.3 6.9 %gather_fusion.2 = f32[1024]{0:T(1024)S(1)} fusion(f32[512]{0:T(512)S(1)} %reshape.207, s32[1024]{0:T(1024)S(1)} %broadcast_clamp_fusion), kind=kCustom, calls=%fused_computation.2 | custom fusion | bytes 12288 | tf_op jit(solution)/shard_map/gather | solution.py:93
  95.2 4.1 %gather_fusion.3 = bf16[1024,1024]{1,0:T(8,128)(2,1)S(1)} fusion(bf16[128,1024]{1,0:T(8,128)(2,1)S(1)} %copy-done.1, s32[1024]{0:T(1024)S(1)} %broadcast_clamp_fusion.1), kind=kCustom, calls=%fused_computation.3 | custom fusion | bytes 4198400 | tf_op jit(solution)/shard_map/gather | solution.py:94
  99.3 1.8 fusion
  101.1 38.2 %all-to-all-done.1 = bf16[64,16,1024]{2,1,0:T(8,128)(2,1)} async-done(((bf16[64,16,1024]{2,1,0:T(8,128)(2,1)}), bf16[64,16,1024]{2,1,0:T(8,128)(2,1)}, u32[]{:S(2)}, u32[]{:S(2)}) %all-to-all-start.1) | async-done | bytes 2097184 | tf_op jit(solution)/shard_map/all_to_all | solution.py:106
  139.3 5.4 %all-to-all-start.4 = ((bf16[64,16,1024]{2,1,0:T(8,128)(2,1)}), bf16[64,16,1024]{2,1,0:T(8,128)(2,1)S(1)}, u32[]{:S(2)}, u32[]{:S(2)}) async-start(bf16[64,16,1024]{2,1,0:T(8,128)(2,1)} %fusion), calls=%async_computation.4 | async-start | bytes 4194304 | tf_op jit(solution)/shard_map/all_to_all | solution.py:112
  144.7 24.9 %all_gather.3 = bf16[1,384,1024]{2,1,0:T(8,128)(2,1)S(1)} all-gather(bf16[1,384,128]{2,1,0:T(8,128)(2,1)} %param.10), channel_id=1, replica_groups=mesh['dp'=8,'expert'=64] {'dp'}, dimensions={2}, use_global_device_ids=true | all-gather | bytes 884736 | tf_op jit(solution)/shard_map/all_gather | solution.py:101
  171.0 5.6 %fusion.13 = f32[1024,768]{0,1:T(8,128)} fusion(bf16[1024,1024]{1,0:T(8,128)(2,1)} %bitcast.5, bf16[1024,768]{1,0:T(8,128)(2,1)} %bitcast.7), kind=kOutput, calls=%fused_computation.56 | convolution fusion | flops 1610612736 | bytes 6815744 | tf_op jit(solution)/shard_map/dot_general | solution.py:9
  176.5 19.4 %all-to-all-done.4 = bf16[64,16,1024]{2,1,0:T(8,128)(2,1)S(1)} async-done(((bf16[64,16,1024]{2,1,0:T(8,128)(2,1)}), bf16[64,16,1024]{2,1,0:T(8,128)(2,1)S(1)}, u32[]{:S(2)}, u32[]{:S(2)}) %all-to-all-start.4) | async-done | bytes 2097184 | tf_op jit(solution)/shard_map/all_to_all | solution.py:112
  195.9 5.0 %multiply_convert_fusion.1 = (bf16[1024,384]{0,1:T(8,128)(2,1)S(1)}, bf16[1024,384]{0,1:T(8,128)(2,1)S(1)}, bf16[1024,384]{0,1:T(8,128)(2,1)}) fusion(f32[1024,768]{0,1:T(8,128)} %fusion.13, bf16[1024,1024]{1,0:T(8,128)(2,1)S(1)} %bitcast.59, bf16[1,384,1024]{2,1,0:T(8,128)(2,1)S(1)} %all_gather.3), kind=kOutput, calls=%fused_computation.18 | convolution fusion | flops 811204608 | bytes 8388608 | tf_op jit(solution)/shard_map/dot_general | solution.py:23
  201.0 5.3 %convert_select_fusion = bf16[1024,1024]{1,0:T(8,128)(2,1)} fusion(pred[1024]{0:T(1024)(128)(4,1)S(1)} %lt.50, bf16[1024,768]{1,0:T(8,128)(2,1)} %bitcast.7, bf16[1024,384]{0,1:T(8,128)(2,1)S(1)} %get-tuple-element.25, bf16[1024,384]{0,1:T(8,128)(2,1)S(1)} %get-tuple-element.24), kind=kOutput, calls=%fused_computation.8 | convolution fusion | flops 1615855616 | bytes 5243904 | tf_op jit(solution)/shard_map/dot_general | solution.py:36
  206.3 5.4 %all-to-all-start.5 = ((bf16[64,16,1024]{2,1,0:T(8,128)(2,1)}), bf16[64,16,1024]{2,1,0:T(8,128)(2,1)S(1)}, u32[]{:S(2)}, u32[]{:S(2)}) async-start(bf16[64,16,1024]{2,1,0:T(8,128)(2,1)} %bitcast.61), calls=%async_computation.5 | async-start | bytes 4194304 | tf_op jit(solution)/shard_map/all_to_all | solution.py:114
  211.8 3.7 %fusion.4 = bf16[1,384,1024]{2,1,0:T(8,128)(2,1)} fusion(bf16[1024,384]{0,1:T(8,128)(2,1)} %get-tuple-element.26, bf16[1024,1024]{1,0:T(8,128)(2,1)} %bitcast.60), kind=kOutput, calls=%fused_computation.24 | convolution fusion | flops 805699584 | bytes 3670016 | tf_op jit(solution)/shard_map/dot_general | solution.py:42
  215.5 4.8 %copy.42 = bf16[1,384,1024]{1,0,2:T(2,128)(2,1)} copy(bf16[1,384,1024]{2,1,0:T(8,128)(2,1)} %fusion.4) | data formatting | bytes 1572864
  220.3 2.5 copy.48
  222.8 3.8 %convert_select_fusion.1 = bf16[1024,1024]{1,0:T(8,128)(2,1)} fusion(pred[1024]{0:T(1024)(128)(4,1)S(1)} %lt.50, bf16[1024,384]{0,1:T(8,128)(2,1)} %get-tuple-element.26, bf16[1,384,1024]{2,1,0:T(8,128)(2,1)S(1)} %all_gather.3), kind=kOutput, calls=%fused_computation.10 | convolution fusion | flops 807403520 | bytes 3671040 | tf_op jit(solution)/shard_map/dot_general | solution.py:13
  226.6 36.4 %all-to-all-done.5 = bf16[64,16,1024]{2,1,0:T(8,128)(2,1)S(1)} async-done(((bf16[64,16,1024]{2,1,0:T(8,128)(2,1)}), bf16[64,16,1024]{2,1,0:T(8,128)(2,1)S(1)}, u32[]{:S(2)}, u32[]{:S(2)}) %all-to-all-start.5) | async-done | bytes 2097184 | tf_op jit(solution)/shard_map/all_to_all | solution.py:114
  263.0 5.7 %all-to-all-start.3 = ((bf16[64,16,1024]{2,1,0:T(8,128)(2,1)}), bf16[64,16,1024]{2,1,0:T(8,128)(2,1)}, u32[]{:S(2)}, u32[]{:S(2)}) async-start(bf16[64,16,1024]{2,1,0:T(8,128)(2,1)} %bitcast.58), calls=%async_computation.3 | async-start | bytes 4194304 | tf_op jit(solution)/shard_map/all_to_all | solution.py:111
  269.0 4.8 %fusion.3 = bf16[1,1024,768]{2,1,0:T(8,128)(2,1)} fusion(bf16[1024,1024]{1,0:T(8,128)(2,1)} %bitcast.5, bf16[1024,384]{0,1:T(8,128)(2,1)} %copy-done.8, bf16[1024,384]{0,1:T(8,128)(2,1)S(1)} %copy-done.7), kind=kOutput, calls=%fused_computation.22 | convolution fusion | flops 1614544896 | bytes 5242880 | tf_op jit(solution)/shard_map/dot_general | solution.py:39
  276.9 37.1 %reduce-scatter.5.cloned.1.call-done = bf16[1,128,768]{2,1,0:T(8,128)(2,1)} async-done(((bf16[1,1024,768]{2,1,0:T(8,128)(2,1)}), bf16[1,128,768]{2,1,0:T(8,128)(2,1)}) %reduce-scatter.5.cloned.1.call-update) | async-done | bytes 196624 | tf_op jit(solution)/shard_map/reduce_scatter | solution.py:116
  314.0 1.7 convert_element_type.78
  315.7 2.8 gather_fusion.4
  318.5 2.3 reshape.208
  320.7 4.6 %gather_fusion.1 = bf16[512,1024]{1,0:T(8,128)(2,1)S(1)} fusion(bf16[1024,1024]{1,0:T(8,128)(2,1)} %bitcast.10, s32[1024]{0:T(1024)S(1)} %pad_clamp_fusion), kind=kCustom, calls=%fused_computation.1 | custom fusion | bytes 2099200 | tf_op jit(solution)/shard_map/gather | solution.py:123
  326.1 3.7 %multiply_reduce_fusion = (f32[128,4]{1,0:T(8,128)S(1)}, bf16[128,1024]{1,0:T(8,128)(2,1)}) fusion(f32[128,4,1024]{2,1,0:T(4,128)S(1)} %reshape.209, f32[128,1024]{1,0:T(8,128)} %convert_element_type.75, f32[128,4]{1,0:T(8,128)S(1)} %copy.34), kind=kLoop, calls=%fused_computation.7 | loop fusion | flops 1965568 | bytes 2887680 | tf_op jit(solution)/shard_map/reduce_sum | solution.py:125
  330.4 2.1 reduce_sum.67
  (59 shorter events, 9.9 us)
Async XLA Ops:
  7.2 34.3 %copy-start = (bf16[128,1024]{1,0:T(8,128)(2,1)S(1)}, bf16[128,1024]{1,0:T(8,128)(2,1)}, u32[]{:S(2)}) copy-start(bf16[128,1024]{1,0:T(8,128)(2,1)} %param.6) | copy-start | bytes 786436
  30.4 50.4 %all-to-all-start.2 = ((bf16[8,1,128,768]{3,2,1,0:T(8,128)(2,1)}), bf16[8,1,128,768]{3,2,1,0:T(8,128)(2,1)}, u32[]{:S(2)}, u32[]{:S(2)}) async-start(bf16[8,1,128,768]{3,2,1,0:T(8,128)(2,1)} %stack.2), calls=%async_computation.2 | async-start | bytes 3145728 | tf_op jit(solution)/shard_map/all_to_all | solution.py:99
  47.1 40.9 %copy-start.5 = (f32[128,4]{0,1:T(4,128)S(1)}, f32[128,4]{0,1:T(4,128)}, u32[]{:S(2)}) copy-start(f32[128,4]{0,1:T(4,128)} %param.8) | copy-start | bytes 6148
  80.8 58.5 %all-to-all-start.1 = ((bf16[64,16,1024]{2,1,0:T(8,128)(2,1)}), bf16[64,16,1024]{2,1,0:T(8,128)(2,1)}, u32[]{:S(2)}, u32[]{:S(2)}) async-start(bf16[64,16,1024]{2,1,0:T(8,128)(2,1)} %broadcast_select_fusion), calls=%async_computation.1 | async-start | bytes 4194304 | tf_op jit(solution)/shard_map/all_to_all | solution.py:106
  88.3 7.0 %copy-start.1 = (bf16[128,1024]{1,0:T(8,128)(2,1)S(1)}, bf16[128,1024]{1,0:T(8,128)(2,1)}, u32[]{:S(2)}) copy-start(bf16[128,1024]{1,0:T(8,128)(2,1)} %param.11) | copy-start | bytes 786436
  139.3 56.7 %all-to-all-start.4 = ((bf16[64,16,1024]{2,1,0:T(8,128)(2,1)}), bf16[64,16,1024]{2,1,0:T(8,128)(2,1)S(1)}, u32[]{:S(2)}, u32[]{:S(2)}) async-start(bf16[64,16,1024]{2,1,0:T(8,128)(2,1)} %fusion), calls=%async_computation.4 | async-start | bytes 4194304 | tf_op jit(solution)/shard_map/all_to_all | solution.py:112
  195.9 5.0 %copy-start.3 = (bf16[64,16,1024]{2,1,0:T(8,128)(2,1)}, bf16[64,16,1024]{2,1,0:T(8,128)(2,1)S(1)}, u32[]{:S(2)}) copy-start(bf16[64,16,1024]{2,1,0:T(8,128)(2,1)S(1)} %all-to-all-done.4) | copy-start | bytes 6291460
  201.0 5.3 %copy-start.6 = (bf16[1024,384]{0,1:T(8,128)(2,1)}, bf16[1024,384]{0,1:T(8,128)(2,1)S(1)}, u32[]{:S(2)}) copy-start(bf16[1024,384]{0,1:T(8,128)(2,1)S(1)} %get-tuple-element.24) | copy-start | bytes 2359300
  201.0 5.3 %copy-start.8 = (bf16[1024,384]{0,1:T(8,128)(2,1)}, bf16[1024,384]{0,1:T(8,128)(2,1)S(1)}, u32[]{:S(2)}) copy-start(bf16[1024,384]{0,1:T(8,128)(2,1)S(1)} %get-tuple-element.25) | copy-start | bytes 2359300
  206.3 56.7 %all-to-all-start.5 = ((bf16[64,16,1024]{2,1,0:T(8,128)(2,1)}), bf16[64,16,1024]{2,1,0:T(8,128)(2,1)S(1)}, u32[]{:S(2)}, u32[]{:S(2)}) async-start(bf16[64,16,1024]{2,1,0:T(8,128)(2,1)} %bitcast.61), calls=%async_computation.5 | async-start | bytes 4194304 | tf_op jit(solution)/shard_map/all_to_all | solution.py:114
  211.7 63.3 %reduce-scatter.7.cloned.1.call-start = ((), (), s32[]{:S(2)}) async-start(), calls=%async_computation.9 | async-start | bytes 884736
  263.0 6.0 %copy-start.7 = (bf16[1024,384]{0,1:T(8,128)(2,1)S(1)}, bf16[1024,384]{0,1:T(8,128)(2,1)}, u32[]{:S(2)}) copy-start(bf16[1024,384]{0,1:T(8,128)(2,1)} %copy-done.6) | copy-start | bytes 2359300
  263.0 57.8 %all-to-all-start.3 = ((bf16[64,16,1024]{2,1,0:T(8,128)(2,1)}), bf16[64,16,1024]{2,1,0:T(8,128)(2,1)}, u32[]{:S(2)}, u32[]{:S(2)}) async-start(bf16[64,16,1024]{2,1,0:T(8,128)(2,1)} %bitcast.58), calls=%async_computation.3 | async-start | bytes 4194304 | tf_op jit(solution)/shard_map/all_to_all | solution.py:111
  268.7 45.3 %reduce-scatter.5.cloned.1.call-start = ((), (), s32[]{:S(2)}) async-start(), calls=%async_computation.8 | async-start | bytes 1769472 | tf_op jit(solution)/shard_map/reduce_scatter | solution.py:116
  273.9 0.9 copy-start.4
  326.1 4.4 %copy-start.2 = (bf16[128,4,1024]{2,1,0:T(4,128)(2,1)S(1)}, bf16[128,4,1024]{2,1,0:T(4,128)(2,1)}, u32[]{:S(2)}) copy-start(bf16[128,4,1024]{2,1,0:T(4,128)(2,1)} %reshape.208) | copy-start | bytes 3145732
Sparse Core Ops, SparseCore 0:
  222.9 37.5 reduce-scatter.6
  274.0 39.9 reduce-scatter.4
